TPU v7x, 512 devices: a whole 4x4x16 slice. The times are simulated.
512 devices in a mesh: req: 128 (over z, x, core), head: 4 (over y).
Axes of the slice: x: 4, y: 4, z: 16, core: 2. Of those that a mesh axis runs over, the one named last changes fastest.
Arguments:
- query_proj: bfloat16 [32768, 2048], P('req', 'head'), may hold values from -6 to 6
- key_proj: bfloat16 [32768, 2048], P('req', 'head'), may hold values from -6 to 6
- value_proj: bfloat16 [32768, 2048], P('req', 'head'), may hold values from -6 to 6
- lengths: int32 [64], replicated, may hold values from 1 to 8, 256 in all
- page_table: int32 [256], P('req'), may hold values from 0 to 255, as said below
- out_weight: bfloat16 [2048, 4096], P('req', 'head'), may hold values from -0.125 to 0.125
- out_bias: float32 [4096], P('head'), may hold values from -3 to 3
Outputs:
- attended: bfloat16 [32768, 4096], P('req', 'head')
- kv_pages: bfloat16 [256, 2, 128, 2048], P('req', None, None, 'head')
Inputs may be any that keep to these rules, and one draw needn't show every extreme that they name: page_table is a permutation in which page b of the stream goes to one of the pages 2 * (b // 2) to 2 * (b // 2) + 1.
All inputs are finite; a program needn't handle non-finite values.
Results may differ from a plain program's by a relative error of at most 0.0046.
Values may be sent and summed in bfloat16 or wider, within the bound.
No kernel may reach another device: no remote copies, remote signals or barrier semaphores. Data moves between devices by JAX's collectives and lax.ppermute only.
A program may use at most 64 MiB of HBM per device.

v0:
```python
import math
import jax
import jax.numpy as jnp
from jax import lax
from jax.sharding import PartitionSpec as P

DH = 128
ROT = 32
PAGE = 128
BLK_DEV = 2
REACH = 4
TOK_DEV = 256
rope_base = 10000.0


def passed_along(array, axis, by):
    count = lax.axis_size(axis)
    pairs = [(i, i + by) for i in range(count) if 0 <= i + by < count]
    return lax.ppermute(array, axis, pairs)


def request_info(lengths, token_index):
    request_ends = jnp.cumsum(lengths) * PAGE
    request_starts = request_ends - lengths * PAGE
    inside = request_starts[None, :] <= token_index[:, None]
    request_id = jnp.sum(inside.astype(jnp.int32), axis=1) - 1
    opening = jnp.max(jnp.where(inside, request_starts[None, :], 0), axis=1)
    return (request_id, token_index - opening)


def rotate_heads(projected, position):
    values_f32 = projected.astype(jnp.float32)
    half_rot = ROT // 2
    frequency = jnp.exp(
        jnp.arange(half_rot, dtype=jnp.float32) * (-2.0 * math.log(rope_base) / ROT)
    )
    angles = position.astype(jnp.float32)[:, None] * frequency[None, :]
    cosine = jnp.cos(angles)[:, None, :]
    sine = jnp.sin(angles)[:, None, :]
    front_half = values_f32[..., :half_rot]
    back_half = values_f32[..., half_rot:ROT]
    turned = jnp.concatenate(
        [
            front_half * cosine - back_half * sine,
            back_half * cosine + front_half * sine,
            values_f32[..., ROT:],
        ],
        axis=-1,
    )
    return turned.astype(jnp.bfloat16)


def attend_block(query_rot, key_rot, value_rows, query_id, query_token, key_id, key_token):
    scores = jnp.einsum("qhd,khd->hqk", query_rot, key_rot, preferred_element_type=jnp.float32) * (
        1.0 / math.sqrt(DH)
    )
    allowed = (query_id[:, None] == key_id[None, :]) & (key_token[None, :] <= query_token[:, None])
    scores = jnp.where(allowed[None], scores, -jnp.inf)
    row_max = jnp.max(scores, axis=-1, keepdims=True)
    raised = jnp.exp(scores - row_max)
    probs = (raised / jnp.sum(raised, axis=-1, keepdims=True)).astype(jnp.bfloat16)
    mixed = jnp.einsum("hqk,khd->qhd", probs, value_rows, preferred_element_type=jnp.float32)
    return mixed.astype(jnp.bfloat16)


def local(query_proj, key_proj, value_proj, lengths, page_table, out_weight, out_bias):
    local_heads = query_proj.shape[1] // DH
    device_rank = lax.axis_index("req")
    first_token = device_rank * TOK_DEV
    own_tokens = first_token + jnp.arange(TOK_DEV, dtype=jnp.int32)
    request_id, position = request_info(lengths, own_tokens)
    query_rot = rotate_heads(query_proj.reshape(TOK_DEV, local_heads, DH), position)
    key_flat = rotate_heads(key_proj.reshape(TOK_DEV, local_heads, DH), position).reshape(
        TOK_DEV, local_heads * DH
    )
    key_list = [key_flat]
    value_list = [value_proj]
    for distance in range(1, REACH + 1):
        far_key, far_value = passed_along((key_flat, value_proj), "req", distance)
        key_list.append(far_key)
        value_list.append(far_value)
    key_stack = jnp.stack(key_list[::-1], axis=0)
    value_stack = jnp.stack(value_list[::-1], axis=0)
    key_rows = (REACH + 1) * TOK_DEV
    key_all = key_stack.reshape(key_rows, local_heads, DH)
    value_all = value_stack.reshape(key_rows, local_heads, DH)
    key_tokens = first_token - REACH * TOK_DEV + jnp.arange(key_rows, dtype=jnp.int32)
    key_id, key_position = request_info(lengths, key_tokens)
    mixed = attend_block(query_rot, key_all, value_all, request_id, own_tokens, key_id, key_tokens)
    heads_out = mixed.reshape(TOK_DEV, local_heads * DH)
    weight_all_rows = lax.all_gather(out_weight, "req", axis=0, tiled=True)
    weight_own_rows = lax.all_to_all(
        weight_all_rows, "head", split_axis=0, concat_axis=1, tiled=True
    )
    partial_value = jnp.dot(heads_out, weight_own_rows, preferred_element_type=jnp.float32)
    summed = lax.psum_scatter(partial_value, "head", scatter_dimension=1, tiled=True)
    attended = (summed + out_bias).astype(jnp.bfloat16)
    local_page = page_table - device_rank * BLK_DEV
    picker = (local_page[:, None] == jnp.arange(BLK_DEV, dtype=jnp.int32)[None, :]).astype(
        jnp.bfloat16
    )
    page_blocks = jnp.stack(
        [
            key_flat.reshape(BLK_DEV, PAGE, local_heads * DH),
            value_proj.reshape(BLK_DEV, PAGE, local_heads * DH),
        ],
        axis=1,
    )
    kv_pages = jnp.einsum(
        "bp,bctd->pctd", picker, page_blocks, preferred_element_type=jnp.float32
    ).astype(jnp.bfloat16)
    return (attended, kv_pages)


def solution(mesh):
    placed = (
        P("req", "head"),
        P("req", "head"),
        P("req", "head"),
        P(),
        P("req"),
        P("req", "head"),
        P("head"),
    )
    return jax.shard_map(
        local,
        mesh=mesh,
        in_specs=placed,
        out_specs=(P("req", "head"), P("req", None, None, "head")),
        check_vma=False,
    )
```

profile of v0, /device:TPU:1, one launch (start us, length us, event | category | flops | bytes accessed | tf_op | source)
XLA Modules:
  0.0 291.5 jit_solution(7986303135102277170)
XLA Ops:
  7.9 0.7 copy.62
  10.0 1.1 copy.68
  12.0 6.2 %collective-permute-start.4 = (bf16[256,512]{0,1:T(8,128)(2,1)S(1)}, bf16[256,512]{0,1:T(8,128)(2,1)}, u32[]{:S(2)}, u32[]{:S(2)}) collective-permute-start(bf16[256,512]{0,1:T(8,128)(2,1)S(1)} %bitcast.44), channel_id=1, source_target_pairs={{0,16},{4,20},{8,24},{12,28},{16,32},{20,36},{24,40},{28,44},{32,4... | collective-permute-start | bytes 786440 | tf_op jit(solution)/shard_map/ppermute | solution.py:19
  18.2 4.3 %collective-permute-start.5 = (bf16[256,512]{0,1:T(8,128)(2,1)S(1)}, bf16[256,512]{0,1:T(8,128)(2,1)}, u32[]{:S(2)}, u32[]{:S(2)}) collective-permute-start(bf16[256,512]{0,1:T(8,128)(2,1)S(1)} %bitcast.45), channel_id=1, source_target_pairs={{0,12},{4,16},{8,20},{12,24},{16,28},{20,32},{24,36},{28,40},{32,4... | collective-permute-start | bytes 786440 | tf_op jit(solution)/shard_map/ppermute | solution.py:19
  22.5 2.4 collective-permute-start.6
  24.9 1.9 collective-permute-start.7
  26.9 5.3 %collective-permute-start = (bf16[256,512]{1,0:T(8,128)(2,1)S(1)}, bf16[256,512]{1,0:T(8,128)(2,1)}, u32[]{:S(2)}, u32[]{:S(2)}) collective-permute-start(bf16[256,512]{1,0:T(8,128)(2,1)S(1)} %copy-done.2), channel_id=1, source_target_pairs={{0,16},{4,20},{8,24},{12,28},{16,32},{20,36},{24,40},{28,44},{32,4... | collective-permute-start | bytes 786440 | tf_op jit(solution)/shard_map/ppermute | solution.py:19
  33.1 135.1 %all-gather.2.cloned.1.call-done = bf16[2048,1024]{1,0:T(8,128)(2,1)} async-done(((bf16[16,1024]{1,0:T(8,128)(2,1)}), bf16[2048,1024]{1,0:T(8,128)(2,1)}) %all-gather.2.cloned.1.call-update) | async-done | bytes 4194320 | tf_op jit(solution)/shard_map/all_gather | solution.py:91
  168.1 4.8 %all-to-all-start = ((bf16[4,512,1024]{2,1,0:T(8,128)(2,1)}), bf16[4,512,1024]{2,1,0:T(8,128)(2,1)}, u32[]{:S(2)}, u32[]{:S(2)}) async-start(bf16[4,512,1024]{2,1,0:T(8,128)(2,1)} %bitcast.43), calls=%async_computation | async-start | bytes 8388608 | tf_op jit(solution)/shard_map/all_to_all | solution.py:92
  173.4 1.0 pad_maximum_fusion.2
  174.4 3.7 %collective-permute-start.1 = (bf16[256,512]{1,0:T(8,128)(2,1)S(1)}, bf16[256,512]{1,0:T(8,128)(2,1)S(1)}, u32[]{:S(2)}, u32[]{:S(2)}) collective-permute-start(bf16[256,512]{1,0:T(8,128)(2,1)S(1)} %copy-done.2), channel_id=1, source_target_pairs={{0,12},{4,16},{8,20},{12,24},{16,28},{20,32},{24,36},{28,40},{32,4... | collective-permute-start | bytes 786440 | tf_op jit(solution)/shard_map/ppermute | solution.py:19
  178.0 1.7 bitcast_dynamic-update-slice_fusion.3
  179.7 2.5 collective-permute-start.2
  182.3 1.0 bitcast_dynamic-update-slice_fusion.8
  183.2 1.9 collective-permute-start.3
  185.2 1.7 bitcast_dynamic-update-slice_fusion.2
  186.8 0.7 bitcast_dynamic-update-slice_fusion.1
  187.6 0.7 bitcast_dynamic-update-slice_fusion
  188.3 0.7 constant_dynamic-update-slice_fusion
  189.1 1.6 copy.73
  190.7 1.3 reshape.211
  192.0 1.0 bitcast_dynamic-update-slice_fusion.6
  193.0 1.0 bitcast_dynamic-update-slice_fusion.5
  194.0 1.3 reshape.209
  195.8 3.1 %exponential_reduce_fusion = f32[4,256]{1,0:T(4,128)S(1)} fusion(bf16[256,4,128]{2,0,1:T(8,128)(2,1)} %pad_maximum_fusion.2, pred[256,1280]{1,0:T(8,128)(4,1)S(1)} %compare_and_fusion, bf16[1280,4,128]{2,1,0:T(4,128)(2,1)S(1)} %copy-done), kind=kOutput, calls=%fused_computation.4 | convolution fusion | flops 340788480 | bytes 1904640 | tf_op jit(solution)/shard_map/sub | solution.py:60
  198.8 4.5 %fusion.5 = bf16[4,128,256]{2,1,0:T(8,128)(2,1)} fusion(f32[4,256]{1,0:T(4,128)S(1)} %exponential_reduce_fusion, bf16[1280,4,128]{2,1,0:T(4,128)(2,1)S(1)} %copy-done.1, bf16[256,4,128]{2,0,1:T(8,128)(2,1)} %pad_maximum_fusion.2, pred[256,1280]{1,0:T(8,128)(4,1)S(1)} %compare_and_fusion, bf16[1280,4,128]{2,1,0:T(4,128)(2,1)S(1)} %copy-done), kind=kOutput, calls=%fused_computation.10 | convolution fusion | flops 677775616 | bytes 3477504 | tf_op jit(solution)/shard_map/hqk,khd->qhd/dot_general | solution.py:62
  203.3 18.3 %all-to-all-done = bf16[4,512,1024]{2,1,0:T(8,128)(2,1)} async-done(((bf16[4,512,1024]{2,1,0:T(8,128)(2,1)}), bf16[4,512,1024]{2,1,0:T(8,128)(2,1)}, u32[]{:S(2)}, u32[]{:S(2)}) %all-to-all-start) | async-done | bytes 4194336 | tf_op jit(solution)/shard_map/all_to_all | solution.py:92
  221.6 6.2 %copy.76 = bf16[512,4,1024]{0,2,1:T(8,128)(2,1)} copy(bf16[512,4,1024]{2,0,1:T(8,128)(2,1)} %bitcast.18) | data formatting | bytes 8388608 | tf_op jit(solution)/shard_map/all_to_all | solution.py:92
  227.9 5.5 %fusion.32 = f32[256,4096]{1,0:T(8,128)} fusion(bf16[256,512]{0,1:T(8,128)(2,1)S(1)} %bitcast.53, bf16[512,4096]{0,1:T(8,128)(2,1)} %bitcast.42), kind=kOutput, calls=%fused_computation.56 | convolution fusion | flops 1073741824 | bytes 8650752 | tf_op jit(solution)/shard_map/dot_general | solution.py:95
  234.8 0.9 copy.80
  235.7 46.8 %reduce-scatter.2.cloned.1.call-done = f32[256,1024]{1,0:T(8,128)} async-done(((f32[256,4096]{1,0:T(8,128)}), f32[256,1024]{1,0:T(8,128)}) %reduce-scatter.2.cloned.1.call-update) | async-done | bytes 1048592 | tf_op jit(solution)/shard_map/reduce_scatter | solution.py:96
  282.5 2.1 add_convert_fusion
  (61 shorter events, 6.1 us)
Async XLA Ops:
  7.2 160.9 %all-gather.2.cloned.1.call-start = ((), (), s32[]{:S(2)}) async-start(), calls=%async_computation.2 | async-start | bytes 4227072 | tf_op jit(solution)/shard_map/all_gather | solution.py:91
  11.5 15.3 %copy-start.2 = (bf16[256,512]{1,0:T(8,128)(2,1)S(1)}, bf16[256,512]{1,0:T(8,128)(2,1)}, u32[]{:S(2)}) copy-start(bf16[256,512]{1,0:T(8,128)(2,1)} %param.9) | copy-start | bytes 786436
  11.6 20.6 %copy-start.4 = (bf16[256,512]{1,0:T(8,128)(2,1)S(1)}, bf16[256,512]{1,0:T(8,128)(2,1)}, u32[]{:S(2)}) copy-start(bf16[256,512]{1,0:T(8,128)(2,1)} %param.7) | copy-start | bytes 786436
  12.0 162.4 %collective-permute-start.4 = (bf16[256,512]{0,1:T(8,128)(2,1)S(1)}, bf16[256,512]{0,1:T(8,128)(2,1)}, u32[]{:S(2)}, u32[]{:S(2)}) collective-permute-start(bf16[256,512]{0,1:T(8,128)(2,1)S(1)} %bitcast.44), channel_id=1, source_target_pairs={{0,16},{4,20},{8,24},{12,28},{16,32},{20,36},{24,40},{28,44},{32,4... | collective-permute-start | bytes 786440 | tf_op jit(solution)/shard_map/ppermute | solution.py:19
  18.2 165.1 %collective-permute-start.5 = (bf16[256,512]{0,1:T(8,128)(2,1)S(1)}, bf16[256,512]{0,1:T(8,128)(2,1)}, u32[]{:S(2)}, u32[]{:S(2)}) collective-permute-start(bf16[256,512]{0,1:T(8,128)(2,1)S(1)} %bitcast.45), channel_id=1, source_target_pairs={{0,12},{4,16},{8,20},{12,24},{16,28},{20,32},{24,36},{28,40},{32,4... | collective-permute-start | bytes 786440 | tf_op jit(solution)/shard_map/ppermute | solution.py:19
  22.5 164.3 %collective-permute-start.6 = (bf16[256,512]{0,1:T(8,128)(2,1)S(1)}, bf16[256,512]{0,1:T(8,128)(2,1)S(1)}, u32[]{:S(2)}, u32[]{:S(2)}) collective-permute-start(bf16[256,512]{0,1:T(8,128)(2,1)S(1)} %bitcast.46), channel_id=1, source_target_pairs={{0,8},{4,12},{8,16},{12,20},{16,24},{20,28},{24,32},{28,36},{32,40... | collective-permute-start | bytes 786440 | tf_op jit(solution)/shard_map/ppermute | solution.py:19
  24.9 162.6 %collective-permute-start.7 = (bf16[256,512]{0,1:T(8,128)(2,1)S(1)}, bf16[256,512]{0,1:T(8,128)(2,1)S(1)}, u32[]{:S(2)}, u32[]{:S(2)}) collective-permute-start(bf16[256,512]{0,1:T(8,128)(2,1)S(1)} %bitcast.47), channel_id=1, source_target_pairs={{0,4},{4,8},{8,12},{12,16},{16,20},{20,24},{24,28},{28,32},{32,36}... | collective-permute-start | bytes 786440 | tf_op jit(solution)/shard_map/ppermute | solution.py:19
  26.9 152.9 %collective-permute-start = (bf16[256,512]{1,0:T(8,128)(2,1)S(1)}, bf16[256,512]{1,0:T(8,128)(2,1)}, u32[]{:S(2)}, u32[]{:S(2)}) collective-permute-start(bf16[256,512]{1,0:T(8,128)(2,1)S(1)} %copy-done.2), channel_id=1, source_target_pairs={{0,16},{4,20},{8,24},{12,28},{16,32},{20,36},{24,40},{28,44},{32,4... | collective-permute-start | bytes 786440 | tf_op jit(solution)/shard_map/ppermute | solution.py:19
  168.1 53.5 %all-to-all-start = ((bf16[4,512,1024]{2,1,0:T(8,128)(2,1)}), bf16[4,512,1024]{2,1,0:T(8,128)(2,1)}, u32[]{:S(2)}, u32[]{:S(2)}) async-start(bf16[4,512,1024]{2,1,0:T(8,128)(2,1)} %bitcast.43), calls=%async_computation | async-start | bytes 8388608 | tf_op jit(solution)/shard_map/all_to_all | solution.py:92
  172.9 109.6 %reduce-scatter.2.cloned.1.call-start = ((), (), s32[]{:S(2)}) async-start(), calls=%async_computation.3 | async-start | bytes 5242880 | tf_op jit(solution)/shard_map/reduce_scatter | solution.py:96
  174.4 14.0 %collective-permute-start.1 = (bf16[256,512]{1,0:T(8,128)(2,1)S(1)}, bf16[256,512]{1,0:T(8,128)(2,1)S(1)}, u32[]{:S(2)}, u32[]{:S(2)}) collective-permute-start(bf16[256,512]{1,0:T(8,128)(2,1)S(1)} %copy-done.2), channel_id=1, source_target_pairs={{0,12},{4,16},{8,20},{12,24},{16,28},{20,32},{24,36},{28,40},{32,4... | collective-permute-start | bytes 786440 | tf_op jit(solution)/shard_map/ppermute | solution.py:19
  179.7 12.2 %collective-permute-start.2 = (bf16[256,512]{1,0:T(8,128)(2,1)S(1)}, bf16[256,512]{1,0:T(8,128)(2,1)}, u32[]{:S(2)}, u32[]{:S(2)}) collective-permute-start(bf16[256,512]{1,0:T(8,128)(2,1)S(1)} %copy-done.2), channel_id=1, source_target_pairs={{0,8},{4,12},{8,16},{12,20},{16,24},{20,28},{24,32},{28,36},{32,40... | collective-permute-start | bytes 786440 | tf_op jit(solution)/shard_map/ppermute | solution.py:19
  183.2 9.7 %collective-permute-start.3 = (bf16[256,512]{1,0:T(8,128)(2,1)S(1)}, bf16[256,512]{1,0:T(8,128)(2,1)}, u32[]{:S(2)}, u32[]{:S(2)}) collective-permute-start(bf16[256,512]{1,0:T(8,128)(2,1)S(1)} %copy-done.2), channel_id=1, source_target_pairs={{0,4},{4,8},{8,12},{12,16},{16,20},{20,24},{24,28},{28,32},{32,36}... | collective-permute-start | bytes 786440 | tf_op jit(solution)/shard_map/ppermute | solution.py:19
  194.0 1.8 copy-start
  195.7 3.1 %copy-start.1 = (bf16[1280,4,128]{2,1,0:T(4,128)(2,1)S(1)}, bf16[1280,4,128]{2,1,0:T(4,128)(2,1)}, u32[]{:S(2)}) copy-start(bf16[1280,4,128]{2,1,0:T(4,128)(2,1)} %reshape.209) | copy-start | bytes 3932164
  221.6 6.2 %copy-start.3 = (bf16[4,128,256]{2,1,0:T(8,128)(2,1)S(1)}, bf16[4,128,256]{2,1,0:T(8,128)(2,1)}, u32[]{:S(2)}) copy-start(bf16[4,128,256]{2,1,0:T(8,128)(2,1)} %fusion.5) | copy-start | bytes 786436
  233.3 0.8 copy-start.6
  234.1 48.4 %copy-start.5 = (f32[1024]{0:T(1024)S(1)}, f32[1024]{0:T(1024)}, u32[]{:S(2)}) copy-start(f32[1024]{0:T(1024)} %param.13) | copy-start | bytes 12292
Sparse Core Ops, SparseCore 0:
  11.1 156.9 all-gather.1
  233.5 49.0 reduce-scatter.1
where the time goes:
time: 292 us; the launch traced here: 291 us
  waiting for transfers between devices  201 us (69%)
  starting transfers between devices  33.2 us (11%)
  local copies, waits for them, and re-layouts  24.1 us (8%)
  between operations  14.4 us (5%)
  matrix products  13.7 us (5%)
  other arithmetic  5.11 us (2%)
    all_gather x1, waiting for transfers between devices, local(): weight_all_rows = lax.all_gather(out_weight, 'req', axis=0, tiled=True)  135 us
    reduce_scatter x1, waiting for transfers between devices, local(): lax.psum_scatter(partial_value, 'head', scatter_dimension=1, tiled=True)  46.8 us
    ppermute x8, starting transfers between devices, passed_along(): return lax.ppermute(array, axis, pairs)  28.3 us
    all_to_all x1, waiting for transfers between devices, local(): lax.all_to_all(weight_all_rows, 'head', split_axis=0, concat_axis=1, tile...  18.3 us
    unnamed x27, local copies, waits for them, and re-layouts  10.7 us
    all_to_all x1, local copies, waits for them, and re-layouts, local(): lax.all_to_all(weight_all_rows, 'head', split_axis=0, concat_axis=1, tile...  6.23 us
  transfers between devices with their start and end apart: 11, of which 3 were waited for; matrix products, arithmetic and copies ran while one was open for 10% of the time, Pallas kernels for 0%

commit v1 on v0

--- a/solution.py
+++ b/solution.py
@@ -88,7 +88,16 @@
     key_id, key_position = request_info(lengths, key_tokens)
     mixed = attend_block(query_rot, key_all, value_all, request_id, own_tokens, key_id, key_tokens)
     heads_out = mixed.reshape(TOK_DEV, local_heads * DH)
-    weight_all_rows = lax.all_gather(out_weight, "req", axis=0, tiled=True)
+    advance_zones = lambda xin, on_dim, which_axis: jnp.concatenate(
+        lax.all_to_all(
+            jnp.stack([xin for _ in range(lax.psum(1, axis_name=which_axis))], axis=0),
+            concat_axis=0,
+            axis_name=which_axis,
+            split_axis=0,
+        ),
+        axis=on_dim,
+    )
+    weight_all_rows = advance_zones(out_weight, 0, "req")
     weight_own_rows = lax.all_to_all(
         weight_all_rows, "head", split_axis=0, concat_axis=1, tiled=True
     )

time: 292 us -> 348 us (1.19)
  waiting for transfers between devices: 201 us -> 231 us
  starting transfers between devices: 33.2 us -> 57.3 us
    all_to_all x0 -> x1, waiting for transfers between devices: none -> 162 us  [local(): lax.all_to_all(jnp.stack([xin for _ in range(lax.psum(1, axis_name=which_...]
    all_gather x1 -> x0, waiting for transfers between devices: 135 us -> none  [local(): weight_all_rows = lax.all_gather(out_weight, 'req', axis=0, tiled=True)]
    all_to_all x0 -> x1, starting transfers between devices: none -> 21 us  [local(): lax.all_to_all(jnp.stack([xin for _ in range(lax.psum(1, axis_name=which_...]
    reduce_scatter x1, waiting for transfers between devices: 46.8 us -> 60.5 us  [local(): lax.psum_scatter(partial_value, 'head', scatter_dimension=1, tiled=True)]
    all_to_all x1, waiting for transfers between devices: 18.3 us -> 8.56 us  [local(): lax.all_to_all(weight_all_rows, 'head', split_axis=0, concat_axis=1, tile...]
    unnamed x27 -> x31, local copies, waits for them, and re-layouts: 10.7 us -> 9.83 us
  transfers between devices with their start and end apart: 11 -> 11, of which waited for: 3 -> 3; matrix products, arithmetic and copies ran while one was open for 10% -> 8% of each run, Pallas kernels for 0% -> 0%
where the time goes in v1:
time: 348 us; the launch traced here: 347 us
  waiting for transfers between devices  231 us (66%)
  starting transfers between devices  57.3 us (16%)
  local copies, waits for them, and re-layouts  25.8 us (7%)
  between operations  14.4 us (4%)
  matrix products  13.7 us (4%)
  other arithmetic  4.45 us (1%)
    all_to_all x1, waiting for transfers between devices, local(): lax.all_to_all(jnp.stack([xin for _ in range(lax.psum(1, axis_name=which_...  162 us
    reduce_scatter x1, waiting for transfers between devices, local(): lax.psum_scatter(partial_value, 'head', scatter_dimension=1, tiled=True)  60.5 us
    ppermute x8, starting transfers between devices, passed_along(): return lax.ppermute(array, axis, pairs)  31.5 us
    all_to_all x1, starting transfers between devices, local(): lax.all_to_all(jnp.stack([xin for _ in range(lax.psum(1, axis_name=which_...  21 us
    unnamed x31, local copies, waits for them, and re-layouts  9.83 us
    all_to_all x1, waiting for transfers between devices, local(): lax.all_to_all(weight_all_rows, 'head', split_axis=0, concat_axis=1, tile...  8.56 us
  transfers between devices with their start and end apart: 11, of which 3 were waited for; matrix products, arithmetic and copies ran while one was open for 8% of the time, Pallas kernels for 0%

profile of v1, /device:TPU:1, one launch (start us, length us, event | category | flops | bytes accessed | tf_op | source)
XLA Modules:
  0.0 346.8 jit_solution(11352651966477247437)
XLA Ops:
  7.2 3.3 stack.37
  10.4 21.0 %all-to-all-start = ((bf16[128,16,1024]{2,1,0:T(8,128)(2,1)}), bf16[128,16,1024]{2,1,0:T(8,128)(2,1)}, u32[]{:S(2)}, u32[]{:S(2)}) async-start(bf16[128,16,1024]{2,1,0:T(8,128)(2,1)} %stack.37), calls=%async_computation | async-start | bytes 8388608 | tf_op jit(solution)/shard_map/all_to_all | solution.py:92
  33.3 5.5 %collective-permute-start.4 = (bf16[256,512]{0,1:T(8,128)(2,1)S(1)}, bf16[256,512]{0,1:T(8,128)(2,1)}, u32[]{:S(2)}, u32[]{:S(2)}) collective-permute-start(bf16[256,512]{0,1:T(8,128)(2,1)S(1)} %bitcast.43), channel_id=1, source_target_pairs={{0,16},{4,20},{8,24},{12,28},{16,32},{20,36},{24,40},{28,44},{32,4... | collective-permute-start | bytes 786440 | tf_op jit(solution)/shard_map/ppermute | solution.py:19
  38.7 3.7 %collective-permute-start.5 = (bf16[256,512]{0,1:T(8,128)(2,1)S(1)}, bf16[256,512]{0,1:T(8,128)(2,1)}, u32[]{:S(2)}, u32[]{:S(2)}) collective-permute-start(bf16[256,512]{0,1:T(8,128)(2,1)S(1)} %bitcast.44), channel_id=1, source_target_pairs={{0,12},{4,16},{8,20},{12,24},{16,28},{20,32},{24,36},{28,40},{32,4... | collective-permute-start | bytes 786440 | tf_op jit(solution)/shard_map/ppermute | solution.py:19
  42.4 2.4 collective-permute-start.6
  44.8 2.2 collective-permute-start.7
  47.0 5.0 %collective-permute-start = (bf16[256,512]{1,0:T(8,128)(2,1)S(1)}, bf16[256,512]{1,0:T(8,128)(2,1)}, u32[]{:S(2)}, u32[]{:S(2)}) collective-permute-start(bf16[256,512]{1,0:T(8,128)(2,1)S(1)} %copy-done.2), channel_id=1, source_target_pairs={{0,16},{4,20},{8,24},{12,28},{16,32},{20,36},{24,40},{28,44},{32,4... | collective-permute-start | bytes 786440 | tf_op jit(solution)/shard_map/ppermute | solution.py:19
  52.9 161.9 %all-to-all-done = bf16[128,16,1024]{2,1,0:T(8,128)(2,1)} async-done(((bf16[128,16,1024]{2,1,0:T(8,128)(2,1)}), bf16[128,16,1024]{2,1,0:T(8,128)(2,1)}, u32[]{:S(2)}, u32[]{:S(2)}) %all-to-all-start) | async-done | bytes 4194336 | tf_op jit(solution)/shard_map/all_to_all | solution.py:92
  214.8 4.8 %all-to-all-start.1 = ((bf16[4,512,1024]{2,1,0:T(8,128)(2,1)}), bf16[4,512,1024]{2,1,0:T(8,128)(2,1)}, u32[]{:S(2)}, u32[]{:S(2)}) async-start(bf16[4,512,1024]{2,1,0:T(8,128)(2,1)} %bitcast.17), calls=%async_computation.1 | async-start | bytes 8388608 | tf_op jit(solution)/shard_map/all_to_all | solution.py:101
  220.1 1.0 pad_maximum_fusion.2
  221.1 7.0 %collective-permute-start.1 = (bf16[256,512]{1,0:T(8,128)(2,1)S(1)}, bf16[256,512]{1,0:T(8,128)(2,1)S(1)}, u32[]{:S(2)}, u32[]{:S(2)}) collective-permute-start(bf16[256,512]{1,0:T(8,128)(2,1)S(1)} %copy-done.2), channel_id=1, source_target_pairs={{0,12},{4,16},{8,20},{12,24},{16,28},{20,32},{24,36},{28,40},{32,4... | collective-permute-start | bytes 786440 | tf_op jit(solution)/shard_map/ppermute | solution.py:19
  228.0 1.7 bitcast_dynamic-update-slice_fusion.3
  229.7 3.7 %collective-permute-start.2 = (bf16[256,512]{1,0:T(8,128)(2,1)S(1)}, bf16[256,512]{1,0:T(8,128)(2,1)}, u32[]{:S(2)}, u32[]{:S(2)}) collective-permute-start(bf16[256,512]{1,0:T(8,128)(2,1)S(1)} %copy-done.2), channel_id=1, source_target_pairs={{0,8},{4,12},{8,16},{12,20},{16,24},{20,28},{24,32},{28,36},{32,40... | collective-permute-start | bytes 786440 | tf_op jit(solution)/shard_map/ppermute | solution.py:19
  233.4 1.0 bitcast_dynamic-update-slice_fusion.8
  234.4 2.1 collective-permute-start.3
  236.5 1.7 bitcast_dynamic-update-slice_fusion.2
  238.2 0.7 bitcast_dynamic-update-slice_fusion.1
  238.9 0.7 bitcast_dynamic-update-slice_fusion
  239.7 0.7 constant_dynamic-update-slice_fusion
  240.4 1.6 copy.73
  242.0 1.3 reshape.215
  243.3 1.0 bitcast_dynamic-update-slice_fusion.6
  244.3 1.0 bitcast_dynamic-update-slice_fusion.5
  245.3 1.3 reshape.213
  247.1 3.1 exponential_reduce_fusion
  250.2 4.5 %fusion.5 = bf16[4,128,256]{2,1,0:T(8,128)(2,1)} fusion(f32[4,256]{1,0:T(4,128)S(1)} %exponential_reduce_fusion, bf16[1280,4,128]{2,1,0:T(4,128)(2,1)S(1)} %copy-done.1, bf16[256,4,128]{2,0,1:T(8,128)(2,1)} %pad_maximum_fusion.2, pred[256,1280]{1,0:T(8,128)(4,1)S(1)} %compare_and_fusion, bf16[1280,4,128]{2,1,0:T(4,128)(2,1)S(1)} %copy-done), kind=kOutput, calls=%fused_computation.10 | convolution fusion | flops 677775616 | bytes 3477504 | tf_op jit(solution)/shard_map/hqk,khd->qhd/dot_general | solution.py:62
  254.6 8.6 %all-to-all-done.1 = bf16[4,512,1024]{2,1,0:T(8,128)(2,1)} async-done(((bf16[4,512,1024]{2,1,0:T(8,128)(2,1)}), bf16[4,512,1024]{2,1,0:T(8,128)(2,1)}, u32[]{:S(2)}, u32[]{:S(2)}) %all-to-all-start.1) | async-done | bytes 4194336 | tf_op jit(solution)/shard_map/all_to_all | solution.py:101
  263.2 6.3 %copy.76 = bf16[512,4,1024]{0,2,1:T(8,128)(2,1)} copy(bf16[512,4,1024]{2,0,1:T(8,128)(2,1)} %bitcast.18) | data formatting | bytes 8388608 | tf_op jit(solution)/shard_map/all_to_all | solution.py:101
  269.4 5.5 %fusion.32 = f32[256,4096]{1,0:T(8,128)} fusion(bf16[256,512]{0,1:T(8,128)(2,1)S(1)} %bitcast.52, bf16[512,4096]{0,1:T(8,128)(2,1)} %bitcast.42), kind=kOutput, calls=%fused_computation.56 | convolution fusion | flops 1073741824 | bytes 8650752 | tf_op jit(solution)/shard_map/dot_general | solution.py:104
  276.4 0.9 copy.80
  277.3 60.5 %reduce-scatter.2.cloned.1.call-done = f32[256,1024]{1,0:T(8,128)} async-done(((f32[256,4096]{1,0:T(8,128)}), f32[256,1024]{1,0:T(8,128)}) %reduce-scatter.2.cloned.1.call-update) | async-done | bytes 1048592 | tf_op jit(solution)/shard_map/reduce_scatter | solution.py:105
  337.8 2.1 add_convert_fusion
  (65 shorter events, 5.0 us)
Async XLA Ops:
  10.4 21.0 %copy-start.7 = (s32[64]{0:T(128)S(1)}, s32[64]{0:T(128)}, u32[]{:S(2)}) copy-start(s32[64]{0:T(128)} %param.10) | copy-start | bytes 772
  10.4 21.8 %copy-start.4 = (bf16[256,512]{1,0:T(8,128)(2,1)S(1)}, bf16[256,512]{1,0:T(8,128)(2,1)}, u32[]{:S(2)}) copy-start(bf16[256,512]{1,0:T(8,128)(2,1)} %param.8) | copy-start | bytes 786436
  10.4 204.4 %all-to-all-start = ((bf16[128,16,1024]{2,1,0:T(8,128)(2,1)}), bf16[128,16,1024]{2,1,0:T(8,128)(2,1)}, u32[]{:S(2)}, u32[]{:S(2)}) async-start(bf16[128,16,1024]{2,1,0:T(8,128)(2,1)} %stack.37), calls=%async_computation | async-start | bytes 8388608 | tf_op jit(solution)/shard_map/all_to_all | solution.py:92
  32.8 14.2 %copy-start.2 = (bf16[256,512]{1,0:T(8,128)(2,1)S(1)}, bf16[256,512]{1,0:T(8,128)(2,1)}, u32[]{:S(2)}) copy-start(bf16[256,512]{1,0:T(8,128)(2,1)} %param.9) | copy-start | bytes 786436
  32.8 19.2 %copy-start.5 = (bf16[256,512]{1,0:T(8,128)(2,1)S(1)}, bf16[256,512]{1,0:T(8,128)(2,1)}, u32[]{:S(2)}) copy-start(bf16[256,512]{1,0:T(8,128)(2,1)} %param.7) | copy-start | bytes 786436
  33.3 187.8 %collective-permute-start.4 = (bf16[256,512]{0,1:T(8,128)(2,1)S(1)}, bf16[256,512]{0,1:T(8,128)(2,1)}, u32[]{:S(2)}, u32[]{:S(2)}) collective-permute-start(bf16[256,512]{0,1:T(8,128)(2,1)S(1)} %bitcast.43), channel_id=1, source_target_pairs={{0,16},{4,20},{8,24},{12,28},{16,32},{20,36},{24,40},{28,44},{32,4... | collective-permute-start | bytes 786440 | tf_op jit(solution)/shard_map/ppermute | solution.py:19
  38.7 195.6 %collective-permute-start.5 = (bf16[256,512]{0,1:T(8,128)(2,1)S(1)}, bf16[256,512]{0,1:T(8,128)(2,1)}, u32[]{:S(2)}, u32[]{:S(2)}) collective-permute-start(bf16[256,512]{0,1:T(8,128)(2,1)S(1)} %bitcast.44), channel_id=1, source_target_pairs={{0,12},{4,16},{8,20},{12,24},{16,28},{20,32},{24,36},{28,40},{32,4... | collective-permute-start | bytes 786440 | tf_op jit(solution)/shard_map/ppermute | solution.py:19
  42.4 195.8 %collective-permute-start.6 = (bf16[256,512]{0,1:T(8,128)(2,1)S(1)}, bf16[256,512]{0,1:T(8,128)(2,1)S(1)}, u32[]{:S(2)}, u32[]{:S(2)}) collective-permute-start(bf16[256,512]{0,1:T(8,128)(2,1)S(1)} %bitcast.45), channel_id=1, source_target_pairs={{0,8},{4,12},{8,16},{12,20},{16,24},{20,28},{24,32},{28,36},{32,40... | collective-permute-start | bytes 786440 | tf_op jit(solution)/shard_map/ppermute | solution.py:19
  44.8 194.1 %collective-permute-start.7 = (bf16[256,512]{0,1:T(8,128)(2,1)S(1)}, bf16[256,512]{0,1:T(8,128)(2,1)S(1)}, u32[]{:S(2)}, u32[]{:S(2)}) collective-permute-start(bf16[256,512]{0,1:T(8,128)(2,1)S(1)} %bitcast.46), channel_id=1, source_target_pairs={{0,4},{4,8},{8,12},{12,16},{16,20},{20,24},{24,28},{28,32},{32,36}... | collective-permute-start | bytes 786440 | tf_op jit(solution)/shard_map/ppermute | solution.py:19
  47.0 182.7 %collective-permute-start = (bf16[256,512]{1,0:T(8,128)(2,1)S(1)}, bf16[256,512]{1,0:T(8,128)(2,1)}, u32[]{:S(2)}, u32[]{:S(2)}) collective-permute-start(bf16[256,512]{1,0:T(8,128)(2,1)S(1)} %copy-done.2), channel_id=1, source_target_pairs={{0,16},{4,20},{8,24},{12,28},{16,32},{20,36},{24,40},{28,44},{32,4... | collective-permute-start | bytes 786440 | tf_op jit(solution)/shard_map/ppermute | solution.py:19
  214.8 48.4 %all-to-all-start.1 = ((bf16[4,512,1024]{2,1,0:T(8,128)(2,1)}), bf16[4,512,1024]{2,1,0:T(8,128)(2,1)}, u32[]{:S(2)}, u32[]{:S(2)}) async-start(bf16[4,512,1024]{2,1,0:T(8,128)(2,1)} %bitcast.17), calls=%async_computation.1 | async-start | bytes 8388608 | tf_op jit(solution)/shard_map/all_to_all | solution.py:101
  219.7 118.2 %reduce-scatter.2.cloned.1.call-start = ((), (), s32[]{:S(2)}) async-start(), calls=%async_computation.3 | async-start | bytes 5242880 | tf_op jit(solution)/shard_map/reduce_scatter | solution.py:105
  221.1 18.6 %collective-permute-start.1 = (bf16[256,512]{1,0:T(8,128)(2,1)S(1)}, bf16[256,512]{1,0:T(8,128)(2,1)S(1)}, u32[]{:S(2)}, u32[]{:S(2)}) collective-permute-start(bf16[256,512]{1,0:T(8,128)(2,1)S(1)} %copy-done.2), channel_id=1, source_target_pairs={{0,12},{4,16},{8,20},{12,24},{16,28},{20,32},{24,36},{28,40},{32,4... | collective-permute-start | bytes 786440 | tf_op jit(solution)/shard_map/ppermute | solution.py:19
  229.7 13.6 %collective-permute-start.2 = (bf16[256,512]{1,0:T(8,128)(2,1)S(1)}, bf16[256,512]{1,0:T(8,128)(2,1)}, u32[]{:S(2)}, u32[]{:S(2)}) collective-permute-start(bf16[256,512]{1,0:T(8,128)(2,1)S(1)} %copy-done.2), channel_id=1, source_target_pairs={{0,8},{4,12},{8,16},{12,20},{16,24},{20,28},{24,32},{28,36},{32,40... | collective-permute-start | bytes 786440 | tf_op jit(solution)/shard_map/ppermute | solution.py:19
  234.4 9.9 %collective-permute-start.3 = (bf16[256,512]{1,0:T(8,128)(2,1)S(1)}, bf16[256,512]{1,0:T(8,128)(2,1)}, u32[]{:S(2)}, u32[]{:S(2)}) collective-permute-start(bf16[256,512]{1,0:T(8,128)(2,1)S(1)} %copy-done.2), channel_id=1, source_target_pairs={{0,4},{4,8},{8,12},{12,16},{16,20},{20,24},{24,28},{28,32},{32,36}... | collective-permute-start | bytes 786440 | tf_op jit(solution)/shard_map/ppermute | solution.py:19
  245.3 1.8 copy-start
  247.1 3.1 copy-start.1
  263.2 6.3 %copy-start.3 = (bf16[4,128,256]{2,1,0:T(8,128)(2,1)S(1)}, bf16[4,128,256]{2,1,0:T(8,128)(2,1)}, u32[]{:S(2)}) copy-start(bf16[4,128,256]{2,1,0:T(8,128)(2,1)} %fusion.5) | copy-start | bytes 786436
  274.9 0.8 copy-start.8
  275.7 62.1 %copy-start.6 = (f32[1024]{0:T(1024)S(1)}, f32[1024]{0:T(1024)}, u32[]{:S(2)}) copy-start(f32[1024]{0:T(1024)} %param.13) | copy-start | bytes 12292
Sparse Core Ops, SparseCore 0:
  275.1 62.7 reduce-scatter.1
